TPU v7x, 32 devices: a whole 2x2x4 slice. The times are simulated.
32 devices in a mesh: lon: 4 (over x, core), lat: 8 (over z, y).
Axes of the slice: x: 2, y: 2, z: 4, core: 2. Of those that a mesh axis runs over, the one named last changes fastest.
Arguments:
- prognostic: float32 [4, 16, 192, 1536], P(None, None, 'lat', 'lon'), may hold values from -6 to 6
- tracers: float32 [4, 16, 192, 1536], P(None, None, 'lat', 'lon'), may hold values from -6 to 6
- zonal_courant: float32 [16, 192, 1536], P(None, 'lat', 'lon'), may hold values from -0.45 to 0.45
- meridional_courant: float32 [16, 192, 1536], P(None, 'lat', 'lon'), may hold values from -0.45 to 0.45
- filter_band: int32 [192], P('lat'), may hold values from 96 to 768, as said below
- dep_owner: int32 [192, 2], P('lat'), may hold values from 0 to 7, as said below
- dep_row: int32 [192, 2], P('lat'), may hold values from 0 to 23
- dep_weight: float32 [192, 2], P('lat'), may hold values from 0 to 1, as said below
Outputs:
- new_prognostic: float32 [4, 16, 192, 1536], P(None, None, 'lat', 'lon')
- new_tracers: float32 [4, 16, 192, 1536], P(None, None, 'lat', 'lon')
Inputs may be any that keep to these rules, and one draw needn't show every extreme that they name: `filter_band`: rows within 24 of either pole hold values below 768; all other rows hold 768. `dep_owner`: among the 48 entries of one band, at most 12 name the same owner band, and some owner is named exactly 12 times; the owners a band names are the bands nearest to it, distance counted across either pole. `dep_weight`: Positive; the 2 weights of a row sum to 1.
All inputs are finite; a program needn't handle non-finite values.
Results may differ from a plain program's by a relative error of at most 0.00007.
Values sent between devices are 32-bit elements; how exact they have to be, the bound alone decides.
No kernel may reach another device: no remote copies, remote signals or barrier semaphores. Data moves between devices by JAX's collectives and lax.ppermute only.
A program may use at most 128 MiB of HBM per device.

v0:
```python
import math
import jax
import jax.numpy as jnp
from jax import lax
from jax.sharding import PartitionSpec as P

PRECISE = lax.Precision.HIGHEST


def padded(value, sides, width, wrap):
    for axis, dim in sides:
        size, length = (lax.axis_size(axis), value.shape[dim])
        up = [(i, (i + 1) % size) for i in range(size if wrap else size - 1)]
        down = [(j, i) for i, j in up]
        last = lax.slice_in_dim(value, length - width, length, axis=dim)
        first = lax.slice_in_dim(value, 0, width, axis=dim)
        before = lax.ppermute(last, axis, up)
        after = lax.ppermute(first, axis, down)
        value = jnp.concatenate([before, value, after], axis=dim)
    return value


def face_flux(values, speeds, axis):
    count = values.shape[axis] - 2
    left_cells = lax.slice_in_dim(values, 0, count + 1, axis=axis)
    right_cells = lax.slice_in_dim(values, 1, count + 2, axis=axis)
    courant = lax.slice_in_dim(speeds, 0, count + 1, axis=axis)
    return 0.5 * courant * (left_cells + right_cells) - 0.5 * courant * courant * (
        right_cells - left_cells
    )


def column_factors(band_rows, length):
    column = jnp.arange(length, dtype=jnp.int32)
    half_length = length // 2
    frequency = jnp.where(column <= half_length, column, column - half_length)
    single = (column == 0) | (column == half_length)
    weights = jnp.where(single, 1.0 / length, 2.0 / length).astype(jnp.float32)
    ratios = (
        band_rows.astype(jnp.float32)[:, None]
        / jnp.maximum(frequency, 1).astype(jnp.float32)[None, :]
    )
    damping = jnp.minimum(1.0, ratios * ratios)
    return (damping - 1.0) * weights[None, :]


def circle_basis(length):
    half_length = length // 2
    column = jnp.arange(length, dtype=jnp.int32)
    frequency = jnp.where(column <= half_length, column, column - half_length)
    low_count = 64
    high_count = length // low_count
    low = jnp.arange(low_count, dtype=jnp.int32)
    high = jnp.arange(high_count, dtype=jnp.int32) * low_count
    scale = 2.0 * math.pi / length
    low_angle = scale * (low[:, None] * frequency[None, :] % length).astype(jnp.float32)
    high_angle = scale * (high[:, None] * frequency[None, :] % length).astype(jnp.float32)
    low_cos, low_sin = (jnp.cos(low_angle), jnp.sin(low_angle))
    high_cos, high_sin = (jnp.cos(high_angle), jnp.sin(high_angle))
    cos_part = high_cos[:, None] * low_cos[None] - high_sin[:, None] * low_sin[None]
    sin_part = high_sin[:, None] * low_cos[None] + high_cos[:, None] * low_sin[None]
    basis = jnp.where((column <= half_length)[None, None, :], cos_part, sin_part)
    return basis.reshape(length, length)


def polar_filter(values, band_rows):
    fields, levels, rows, block_cells = values.shape
    parts = lax.axis_size("lon")
    length = block_cells * parts
    flat = values.reshape(fields * levels * rows, block_cells)
    circles = lax.all_to_all(flat, "lon", split_axis=0, concat_axis=1, tiled=True)
    basis_table = circle_basis(length)
    spectrum = jnp.dot(circles, basis_table, precision=PRECISE)
    factors = column_factors(band_rows, length)
    circle_rows = circles.shape[0]
    scaled = (spectrum.reshape(circle_rows // rows, rows, length) * factors[None]).reshape(
        circle_rows, length
    )
    change = lax.dot_general(scaled, basis_table, (((1,), (1,)), ((), ())), precision=PRECISE)
    back = lax.all_to_all(change, "lon", split_axis=1, concat_axis=0, tiled=True)
    return values + back.reshape(values.shape)


def departure_terms(tracers, dep_owner, dep_row, dep_weight):
    band_count = lax.axis_size("lat")
    row_count, link_count = dep_owner.shape
    entries = row_count * link_count
    capacity = max(2, -(-2 * entries // band_count))
    owner_ids = dep_owner.reshape(entries)
    source = dep_row.reshape(entries)
    positions = jnp.arange(entries)
    earlier = (owner_ids[:, None] == owner_ids[None, :]) & (positions[None, :] < positions[:, None])
    slot_ids = jnp.sum(earlier.astype(jnp.int32), axis=1)
    band_ids = jnp.arange(band_count, dtype=jnp.int32)
    slot_range = jnp.arange(capacity, dtype=jnp.int32)
    matches = (owner_ids[:, None, None] == band_ids[None, :, None]) & (
        slot_ids[:, None, None] == slot_range[None, None, :]
    )
    request = jnp.sum(jnp.where(matches, source[:, None, None], 0), axis=0)
    wanted = lax.all_to_all(request, "lat", split_axis=0, concat_axis=0, tiled=True)
    by_row = jnp.transpose(tracers, (2, 0, 1, 3))
    outgoing = by_row[wanted]
    incoming = lax.all_to_all(outgoing, "lat", split_axis=0, concat_axis=0, tiled=True)
    stacked_rows = incoming.reshape((band_count * capacity,) + incoming.shape[2:])
    picked = stacked_rows[owner_ids * capacity + slot_ids].reshape(
        (row_count, link_count) + stacked_rows.shape[1:]
    )
    summed = dep_weight[:, 0][:, None, None, None] * picked[:, 0]
    summed = summed + dep_weight[:, 1][:, None, None, None] * picked[:, 1]
    return jnp.transpose(summed, (1, 2, 0, 3))


def body(
    prognostic,
    tracers,
    zonal_courant,
    meridional_courant,
    filter_band,
    dep_owner,
    dep_row,
    dep_weight,
):
    row_count = prognostic.shape[2]
    departed = departure_terms(tracers, dep_owner, dep_row, dep_weight)
    lon_padded = padded(
        jnp.concatenate([prognostic, zonal_courant[None]], axis=0), (("lon", 3),), 1, True
    )
    zonal_flux = face_flux(lon_padded[:-1], lon_padded[-1:], 3)
    lat_padded = padded(
        jnp.concatenate([prognostic, meridional_courant[None]], axis=0), (("lat", 2),), 1, False
    )
    merid_flux = face_flux(lat_padded[:-1], lat_padded[-1:], 2)
    total_rows = row_count * lax.axis_size("lat")
    face_rows = lax.axis_index("lat") * row_count + jnp.arange(row_count + 1) - 1
    merid_flux = jnp.where(
        (face_rows == total_rows - 1)[None, None, :, None], jnp.float32(0.0), merid_flux
    )
    advected = (
        prognostic
        - (zonal_flux[..., 1:] - zonal_flux[..., :-1])
        - (merid_flux[:, :, 1:] - merid_flux[:, :, :-1])
    )
    new_prognostic = polar_filter(advected, filter_band)
    return (new_prognostic, departed)


def solution(mesh):
    return jax.shard_map(
        body,
        mesh=mesh,
        in_specs=(
            P(None, None, "lat", "lon"),
            P(None, None, "lat", "lon"),
            P(None, "lat", "lon"),
            P(None, "lat", "lon"),
            P("lat"),
            P("lat", None),
            P("lat", None),
            P("lat", None),
        ),
        out_specs=(P(None, None, "lat", "lon"), P(None, None, "lat", "lon")),
        check_vma=False,
    )
```

profile of v0, /device:TPU:0, one launch (start us, length us, event | category | flops | bytes accessed | tf_op | source)
XLA Modules:
  0.0 364.4 jit_solution(3108932577473310589)
XLA Ops:
  0.7 3.3 pad_maximum_fusion.8
  10.8 4.9 %collective-permute-start.2 = (f32[5,16,1,384]{3,1,2,0:T(8,128)}, f32[5,16,1,384]{3,1,2,0:T(8,128)}, u32[]{:S(2)}, u32[]{:S(2)}) collective-permute-start(f32[5,16,1,384]{3,1,2,0:T(8,128)} %copy.61), channel_id=1, source_target_pairs={{0,1},{1,2},{2,3},{3,4},{4,5},{5,6},{6,7},{8,9},{9,10},{10,11},{11... | collective-permute-start | bytes 368648 | tf_op jit(solution)/shard_map/ppermute | solution.py:17
  20.8 2.2 multiply_bitcast_fusion.1
  24.0 2.3 copy.60
  26.3 2.7 multiply_subtract_fusion
  32.6 2.3 fusion.4
  34.9 3.6 all-to-all-start
  41.5 5.8 %add_select_fusion = f32[24,64,1536]{2,1,0:T(8,128)} fusion(f32[64,1536]{1,0:T(8,128)S(1)} %get-tuple-element.21, f32[24,1536]{1,0:T(8,128)S(1)} %get-tuple-element.19, f32[64,1536]{1,0:T(8,128)S(1)} %get-tuple-element.20, f32[24,1536]{1,0:T(8,128)S(1)} %get-tuple-element.18, pred[1536]{0:T(1024)(128)(4,1)S(1)} %iota_compare_fusion.4), kind=kLoop, calls=%fused_computation.2 | loop fusion | flops 16515072 | bytes 10520064 | tf_op jit(solution)/shard_map/jit(_where)/select_n | solution.py:62
  47.3 19.7 %all-to-all-done = f32[4,384,384]{2,1,0:T(8,128)S(1)} async-done(((f32[4,384,384]{2,1,0:T(8,128)}), f32[4,384,384]{2,1,0:T(8,128)S(1)}, u32[]{:S(2)}, u32[]{:S(2)}) %all-to-all-start) | async-done | bytes 2359328 | tf_op jit(solution)/shard_map/all_to_all | solution.py:71
  67.0 6.9 %all-to-all-start.2 = ((s32[8,1,12]{2,1,0:T(1,128)}), s32[8,1,12]{2,1,0:T(1,128)S(1)}, u32[]{:S(2)}, u32[]{:S(2)}) async-start(s32[8,1,12]{2,1,0:T(1,128)} %copy.70), calls=%async_computation.2 | async-start | bytes 8192 | tf_op jit(solution)/shard_map/all_to_all | solution.py:100
  73.9 2.9 copy.65
  76.9 2.7 dot_general.8
  79.6 14.7 %convolution_multiply_fusion = f32[16,24,1536]{2,1,0:T(8,128)S(1)} fusion(f32[16,24,1536]{2,1,0:T(8,128)S(1)} %dot_general.8, f32[1536,1536,1]{1,0,2:T(8,128)} %bitcast.64, f32[24,1536]{1,0:T(8,128)S(1)} %fusion.18), kind=kOutput, calls=%fused_computation.13 | convolution fusion | flops 10872225792 | bytes 14303232 | tf_op jit(solution)/shard_map/dot_general | solution.py:73
  94.3 13.0 %fusion.31 = f32[384,4,384]{2,0,1:T(8,128)} fusion(f32[384,1536,1]{1,0,2:T(8,128)S(1)} %bitcast.71, f32[4,384,1536]{2,1,0:T(8,128)S(1)} %bitcast.65), kind=kOutput, calls=%fused_computation.87 | convolution fusion | flops 10871635968 | bytes 14155776 | tf_op jit(solution)/shard_map/dot_general | solution.py:79
  107.3 4.8 %all-to-all-start.1 = ((f32[384,4,384]{2,0,1:T(8,128)}), f32[384,4,384]{2,0,1:T(8,128)}, u32[]{:S(2)}, u32[]{:S(2)}) async-start(f32[384,4,384]{2,0,1:T(8,128)} %fusion.31), calls=%async_computation.1 | async-start | bytes 4718592 | tf_op jit(solution)/shard_map/all_to_all | solution.py:80
  112.1 2.1 copy.78
  114.3 4.8 %gather_fusion = f32[96,4,16,384]{3,2,1,0:T(8,128)} fusion(f32[24,4,16,384]{3,2,1,0:T(8,128)S(1)} %bitcast.66, s32[1024]{0:T(1024)S(1)} %pad_clamp_fusion.1), kind=kCustom, calls=%fused_computation | custom fusion | bytes 18874752 | tf_op jit(solution)/shard_map/gather | solution.py:102
  119.1 21.3 %all-to-all-done.1 = f32[384,4,384]{2,0,1:T(8,128)} async-done(((f32[384,4,384]{2,0,1:T(8,128)}), f32[384,4,384]{2,0,1:T(8,128)}, u32[]{:S(2)}, u32[]{:S(2)}) %all-to-all-start.1) | async-done | bytes 2359328 | tf_op jit(solution)/shard_map/all_to_all | solution.py:80
  140.4 6.1 %all-to-all-start.3 = ((f32[8,12,4,16,384]{4,3,2,1,0:T(8,128)}), f32[8,12,4,16,384]{4,3,2,1,0:T(8,128)}, u32[]{:S(2)}, u32[]{:S(2)}) async-start(f32[8,12,4,16,384]{4,3,2,1,0:T(8,128)} %bitcast.67), calls=%async_computation.3 | async-start | bytes 18874368 | tf_op jit(solution)/shard_map/all_to_all | solution.py:103
  146.8 3.3 add.134
  150.1 201.9 %all-to-all-done.3 = f32[8,12,4,16,384]{4,3,2,1,0:T(8,128)} async-done(((f32[8,12,4,16,384]{4,3,2,1,0:T(8,128)}), f32[8,12,4,16,384]{4,3,2,1,0:T(8,128)}, u32[]{:S(2)}, u32[]{:S(2)}) %all-to-all-start.3) | async-done | bytes 9437216 | tf_op jit(solution)/shard_map/all_to_all | solution.py:103
  352.0 6.7 %gather_fusion.1 = f32[48,4,16,384]{3,2,1,0:T(8,128)} fusion(f32[96,4,16,384]{3,2,1,0:T(8,128)} %bitcast.20, s32[1024]{0:T(1024)S(1)} %pad_clamp_fusion), kind=kCustom, calls=%fused_computation.1 | custom fusion | bytes 9437376 | tf_op jit(solution)/shard_map/gather | solution.py:105
  358.7 2.9 fusion.2
  361.6 2.8 copy.73
  (72 shorter events, 19.6 us)
Async XLA Ops:
  0.6 9.3 %copy-start = (f32[4,16,24,384]{3,2,1,0:T(8,128)S(1)}, f32[4,16,24,384]{3,2,1,0:T(8,128)}, u32[]{:S(2)}) copy-start(f32[4,16,24,384]{3,2,1,0:T(8,128)} %param.8) | copy-start | bytes 7077892
  0.6 9.3 %copy-start.3 = (f32[16,24,384]{2,1,0:T(8,128)S(1)}, f32[16,24,384]{2,1,0:T(8,128)}, u32[]{:S(2)}) copy-start(f32[16,24,384]{2,1,0:T(8,128)} %param.11) | copy-start | bytes 1769476
  4.0 13.7 %copy-start.5 = (s32[24,2]{0,1:T(2,128)S(1)}, s32[24,2]{0,1:T(2,128)}, u32[]{:S(2)}) copy-start(s32[24,2]{0,1:T(2,128)} %param.13) | copy-start | bytes 580
  4.0 14.1 %copy-start.11 = (s32[24]{0:T(128)S(1)}, s32[24]{0:T(128)}, u32[]{:S(2)}) copy-start(s32[24]{0:T(128)} %param.12) | copy-start | bytes 292
  4.0 14.1 %copy-start.7 = (s32[24,2]{0,1:T(2,128)S(1)}, s32[24,2]{0,1:T(2,128)}, u32[]{:S(2)}) copy-start(s32[24,2]{0,1:T(2,128)} %param.14) | copy-start | bytes 580
  5.7 13.8 %collective-permute-start = (f32[5,16,24,1]{2,1,3,0:T(8,128)S(1)}, f32[5,16,24,1]{2,1,3,0:T(8,128)}, u32[]{:S(2)}, u32[]{:S(2)}) collective-permute-start(f32[5,16,24,1]{2,1,3,0:T(8,128)S(1)} %copy.57), channel_id=1, source_target_pairs={{0,8},{8,16},{16,24},{24,0},{1,9},{9,17},{17,25},{25,1},{2,10},{10... | collective-permute-start | bytes 23048 | tf_op jit(solution)/shard_map/ppermute | solution.py:17
  7.9 16.1 %collective-permute-start.1 = (f32[5,16,24,1]{2,1,3,0:T(8,128)S(1)}, f32[5,16,24,1]{2,1,3,0:T(8,128)}, u32[]{:S(2)}, u32[]{:S(2)}) collective-permute-start(f32[5,16,24,1]{2,1,3,0:T(8,128)S(1)} %copy.59), channel_id=1, source_target_pairs={{8,0},{16,8},{24,16},{0,24},{9,1},{17,9},{25,17},{1,25},{10,2},{18... | collective-permute-start | bytes 23048 | tf_op jit(solution)/shard_map/ppermute | solution.py:18
  10.8 18.3 %collective-permute-start.2 = (f32[5,16,1,384]{3,1,2,0:T(8,128)}, f32[5,16,1,384]{3,1,2,0:T(8,128)}, u32[]{:S(2)}, u32[]{:S(2)}) collective-permute-start(f32[5,16,1,384]{3,1,2,0:T(8,128)} %copy.61), channel_id=1, source_target_pairs={{0,1},{1,2},{2,3},{3,4},{4,5},{5,6},{6,7},{8,9},{9,10},{10,11},{11... | collective-permute-start | bytes 368648 | tf_op jit(solution)/shard_map/ppermute | solution.py:17
  16.3 14.1 %collective-permute-start.3 = (f32[5,16,1,384]{3,1,2,0:T(8,128)}, f32[5,16,1,384]{3,1,2,0:T(8,128)}, u32[]{:S(2)}, u32[]{:S(2)}) collective-permute-start(f32[5,16,1,384]{3,1,2,0:T(8,128)} %copy.63), channel_id=1, source_target_pairs={{1,0},{2,1},{3,2},{4,3},{5,4},{6,5},{7,6},{9,8},{10,9},{11,10},{12... | collective-permute-start | bytes 368648 | tf_op jit(solution)/shard_map/ppermute | solution.py:18
  18.0 0.6 copy-start.9
  26.3 3.8 %copy-start.4 = (f32[16,24,384]{2,1,0:T(8,128)S(1)}, f32[16,24,384]{2,1,0:T(8,128)}, u32[]{:S(2)}) copy-start(f32[16,24,384]{2,1,0:T(8,128)} %param.11) | copy-start | bytes 1769476
  30.1 1.3 copy-start.8
  34.9 32.1 %all-to-all-start = ((f32[4,384,384]{2,1,0:T(8,128)}), f32[4,384,384]{2,1,0:T(8,128)S(1)}, u32[]{:S(2)}, u32[]{:S(2)}) async-start(f32[4,384,384]{2,1,0:T(8,128)} %bitcast.68), calls=%async_computation | async-start | bytes 4718592 | tf_op jit(solution)/shard_map/all_to_all | solution.py:71
  67.0 40.3 %all-to-all-start.2 = ((s32[8,1,12]{2,1,0:T(1,128)}), s32[8,1,12]{2,1,0:T(1,128)S(1)}, u32[]{:S(2)}, u32[]{:S(2)}) async-start(s32[8,1,12]{2,1,0:T(1,128)} %copy.70), calls=%async_computation.2 | async-start | bytes 8192 | tf_op jit(solution)/shard_map/all_to_all | solution.py:100
  79.6 14.8 %copy-start.1 = (f32[24,64,1536]{2,1,0:T(8,128)S(1)}, f32[24,64,1536]{2,1,0:T(8,128)}, u32[]{:S(2)}) copy-start(f32[24,64,1536]{2,1,0:T(8,128)} %add_select_fusion) | copy-start | bytes 28311556
  107.3 33.1 %all-to-all-start.1 = ((f32[384,4,384]{2,0,1:T(8,128)}), f32[384,4,384]{2,0,1:T(8,128)}, u32[]{:S(2)}, u32[]{:S(2)}) async-start(f32[384,4,384]{2,0,1:T(8,128)} %fusion.31), calls=%async_computation.1 | async-start | bytes 4718592 | tf_op jit(solution)/shard_map/all_to_all | solution.py:80
  140.4 6.3 %copy-start.10 = (s32[48]{0:T(128)S(1)}, s32[48]{0:T(128)}, u32[]{:S(2)}) copy-start(s32[48]{0:T(128)} %copy-done.9) | copy-start | bytes 580
  140.4 6.4 %copy-start.6 = (f32[24,2]{0,1:T(2,128)S(1)}, f32[24,2]{0,1:T(2,128)}, u32[]{:S(2)}) copy-start(f32[24,2]{0,1:T(2,128)} %param.15) | copy-start | bytes 580
  140.4 6.4 %copy-start.2 = (f32[4,16,24,384]{3,2,1,0:T(8,128)S(1)}, f32[4,16,24,384]{3,2,1,0:T(8,128)}, u32[]{:S(2)}) copy-start(f32[4,16,24,384]{3,2,1,0:T(8,128)} %fusion.4) | copy-start | bytes 7077892
  140.4 211.6 %all-to-all-start.3 = ((f32[8,12,4,16,384]{4,3,2,1,0:T(8,128)}), f32[8,12,4,16,384]{4,3,2,1,0:T(8,128)}, u32[]{:S(2)}, u32[]{:S(2)}) async-start(f32[8,12,4,16,384]{4,3,2,1,0:T(8,128)} %bitcast.67), calls=%async_computation.3 | async-start | bytes 18874368 | tf_op jit(solution)/shard_map/all_to_all | solution.py:103
where the time goes:
time: 365 us; the launch traced here: 364 us
  waiting for transfers between devices  243 us (67%)
  local copies, waits for them, and re-layouts  34.2 us (9%)
  starting transfers between devices  30.1 us (8%)
  other arithmetic  28.6 us (8%)
  matrix products  27.7 us (8%)
    all_to_all x1, waiting for transfers between devices, departure_terms(): lax.all_to_all(outgoing, 'lat', split_axis=0, concat_axis=0, tiled=True)  202 us
    all_to_all x1, waiting for transfers between devices, polar_filter(): lax.all_to_all(change, 'lon', split_axis=1, concat_axis=0, tiled=True)  21.3 us
    all_to_all x1, waiting for transfers between devices, polar_filter(): lax.all_to_all(flat, 'lon', split_axis=0, concat_axis=1, tiled=True)  19.7 us
    dot_general x1, matrix products, polar_filter(): spectrum = jnp.dot(circles, basis_table, precision=PRECISE)  14.7 us
    dot_general x1, matrix products, polar_filter(): lax.dot_general(scaled, basis_table, (((1,), (1,)), ((), ())), precision=...  13 us
  transfers between devices with their start and end apart: 8, of which 3 were waited for; matrix products, arithmetic and copies ran while one was open for 19% of the time, Pallas kernels for 0%

commit v1 on v0

--- a/solution.py
+++ b/solution.py
@@ -5,6 +5,22 @@
 from jax.sharding import PartitionSpec as P
 
 PRECISE = lax.Precision.HIGHEST
+
+
+def pairwise_exchange(value, axis, split, join):
+    ways, here = (lax.axis_size(axis), lax.axis_index(axis))
+    width = value.shape[split] // ways
+    shape = list(value.shape)
+    shape[split] = width
+    height = shape[join]
+    shape[join] = height * ways
+    full = jnp.zeros(shape, value.dtype)
+    for mask in range(ways):
+        part = lax.dynamic_slice_in_dim(value, (here ^ mask) * width, width, axis=split)
+        if mask:
+            part = lax.ppermute(part, axis, [(d, d ^ mask) for d in range(ways)])
+        full = lax.dynamic_update_slice_in_dim(full, part, (here ^ mask) * height, axis=join)
+    return full
 
 
 def padded(value, sides, width, wrap):
@@ -97,7 +113,7 @@
         slot_ids[:, None, None] == slot_range[None, None, :]
     )
     request = jnp.sum(jnp.where(matches, source[:, None, None], 0), axis=0)
-    wanted = lax.all_to_all(request, "lat", split_axis=0, concat_axis=0, tiled=True)
+    wanted = pairwise_exchange(request, "lat", 0, 0)
     by_row = jnp.transpose(tracers, (2, 0, 1, 3))
     outgoing = by_row[wanted]
     incoming = lax.all_to_all(outgoing, "lat", split_axis=0, concat_axis=0, tiled=True)

time: 365 us -> 358 us (0.981)
  waiting for transfers between devices: 243 us -> 230 us
  starting transfers between devices: 30.1 us -> 36.8 us
    all_to_all x1, waiting for transfers between devices: 21.3 us -> 1.29 us  [polar_filter(): lax.all_to_all(change, 'lon', split_axis=1, concat_axis=0, tiled=True)]
    ppermute x0 -> x7, starting transfers between devices: none -> 12.5 us  [pairwise_exchange(): part = lax.ppermute(part, axis, [(d, d ^ mask) for d in range(ways)])]
    all_to_all x1 -> x0, starting transfers between devices: 6.94 us -> none  [departure_terms(): lax.all_to_all(request, 'lat', split_axis=0, concat_axis=0, tiled=True)]
    ppermute x0 -> x7, waiting for transfers between devices: none -> 5.53 us  [pairwise_exchange(): part = lax.ppermute(part, axis, [(d, d ^ mask) for d in range(ways)])]
  transfers between devices with their start and end apart: 8 -> 14, of which waited for: 3 -> 6; matrix products, arithmetic and copies ran while one was open for 19% -> 10% of each run, Pallas kernels for 0% -> 0%
where the time goes in v1:
time: 358 us; the launch traced here: 357 us
  waiting for transfers between devices  230 us (64%)
  starting transfers between devices  36.8 us (10%)
  local copies, waits for them, and re-layouts  33.6 us (9%)
  other arithmetic  27.7 us (8%)
  matrix products  27.7 us (8%)
    all_to_all x1, waiting for transfers between devices, departure_terms(): lax.all_to_all(outgoing, 'lat', split_axis=0, concat_axis=0, tiled=True)  202 us
    all_to_all x1, waiting for transfers between devices, polar_filter(): lax.all_to_all(flat, 'lon', split_axis=0, concat_axis=1, tiled=True)  20.2 us
    dot_general x1, matrix products, polar_filter(): spectrum = jnp.dot(circles, basis_table, precision=PRECISE)  14.7 us
    dot_general x1, matrix products, polar_filter(): lax.dot_general(scaled, basis_table, (((1,), (1,)), ((), ())), precision=...  13 us
    ppermute x7, starting transfers between devices, pairwise_exchange(): part = lax.ppermute(part, axis, [(d, d ^ mask) for d in range(ways)])  12.5 us
  transfers between devices with their start and end apart: 14, of which 6 were waited for; matrix products, arithmetic and copies ran while one was open for 10% of the time, Pallas kernels for 0%

profile of v1, /device:TPU:0, one launch (start us, length us, event | category | flops | bytes accessed | tf_op | source)
XLA Modules:
  0.0 357.1 jit_solution(9751716284253255025)
XLA Ops:
  3.2 5.5 %collective-permute-start.2 = (f32[5,16,1,384]{3,1,2,0:T(8,128)}, f32[5,16,1,384]{3,1,2,0:T(8,128)}, u32[]{:S(2)}, u32[]{:S(2)}) collective-permute-start(f32[5,16,1,384]{3,1,2,0:T(8,128)} %copy.59), channel_id=1, source_target_pairs={{0,1},{1,2},{2,3},{3,4},{4,5},{5,6},{6,7},{8,9},{9,10},{10,11},{11... | collective-permute-start | bytes 368648 | tf_op jit(solution)/shard_map/ppermute | solution.py:33
  12.0 2.4 copy.55
  22.6 2.3 copy.58
  24.8 2.7 multiply_subtract_fusion
  31.1 2.3 fusion.4
  33.4 3.8 %all-to-all-start = ((f32[4,384,384]{2,1,0:T(8,128)}), f32[4,384,384]{2,1,0:T(8,128)S(1)}, u32[]{:S(2)}, u32[]{:S(2)}) async-start(f32[4,384,384]{2,1,0:T(8,128)} %bitcast.64), calls=%async_computation | async-start | bytes 4718592 | tf_op jit(solution)/shard_map/all_to_all | solution.py:87
  39.5 5.8 %add_select_fusion = f32[24,64,1536]{2,1,0:T(8,128)} fusion(f32[64,1536]{1,0:T(8,128)S(1)} %get-tuple-element.29, f32[24,1536]{1,0:T(8,128)S(1)} %get-tuple-element.19, f32[64,1536]{1,0:T(8,128)S(1)} %get-tuple-element.28, f32[24,1536]{1,0:T(8,128)S(1)} %get-tuple-element.18, pred[1536]{0:T(1024)(128)(4,1)S(1)} %iota_compare_fusion.4), kind=kLoop, calls=%fused_computation.2 | loop fusion | flops 16515072 | bytes 10520064 | tf_op jit(solution)/shard_map/jit(_where)/select_n | solution.py:78
  45.3 20.2 %all-to-all-done = f32[4,384,384]{2,1,0:T(8,128)S(1)} async-done(((f32[4,384,384]{2,1,0:T(8,128)}), f32[4,384,384]{2,1,0:T(8,128)S(1)}, u32[]{:S(2)}, u32[]{:S(2)}) %all-to-all-start) | async-done | bytes 2359328 | tf_op jit(solution)/shard_map/all_to_all | solution.py:87
  65.5 2.9 copy.63
  68.5 2.7 dot_general.8
  71.2 14.7 %convolution_multiply_fusion = f32[16,24,1536]{2,1,0:T(8,128)S(1)} fusion(f32[16,24,1536]{2,1,0:T(8,128)S(1)} %dot_general.8, f32[1536,1536,1]{1,0,2:T(8,128)} %bitcast.60, f32[24,1536]{1,0:T(8,128)S(1)} %fusion.18), kind=kOutput, calls=%fused_computation.13 | convolution fusion | flops 10872225792 | bytes 14303232 | tf_op jit(solution)/shard_map/dot_general | solution.py:89
  85.9 13.0 %fusion.31 = f32[384,4,384]{2,0,1:T(8,128)} fusion(f32[384,1536,1]{1,0,2:T(8,128)S(1)} %bitcast.67, f32[4,384,1536]{2,1,0:T(8,128)S(1)} %bitcast.61), kind=kOutput, calls=%fused_computation.95 | convolution fusion | flops 10871635968 | bytes 14155776 | tf_op jit(solution)/shard_map/dot_general | solution.py:95
  98.9 4.9 %all-to-all-start.1 = ((f32[384,4,384]{2,0,1:T(8,128)}), f32[384,4,384]{2,0,1:T(8,128)}, u32[]{:S(2)}, u32[]{:S(2)}) async-start(f32[384,4,384]{2,0,1:T(8,128)} %fusion.31), calls=%async_computation.1 | async-start | bytes 4718592 | tf_op jit(solution)/shard_map/all_to_all | solution.py:96
  104.9 2.7 collective-permute-start.4
  109.3 3.0 collective-permute-start.7
  115.7 3.6 %collective-permute-start.9 = (s32[1,12]{0,1:T(8,128)S(1)}, s32[1,12]{0,1:T(8,128)S(1)}, u32[]{:S(2)}, u32[]{:S(2)}) collective-permute-start(s32[1,12]{0,1:T(8,128)S(1)} %get-tuple-element.21), channel_id=1, source_target_pairs={{0,6},{1,7},{2,4},{3,5},{4,2},{5,3},{6,0},{7,1},{8,14},{9,15},{10,... | collective-permute-start | bytes 152 | tf_op jit(solution)/shard_map/ppermute | solution.py:21
  121.3 4.5 %collective-permute-done.10 = s32[1,12]{0,1:T(8,128)S(1)} collective-permute-done((s32[1,12]{0,1:T(8,128)S(1)}, s32[1,12]{0,1:T(8,128)S(1)}, u32[]{:S(2)}, u32[]{:S(2)}) %collective-permute-start.10) | collective-permute-done | bytes 80 | tf_op jit(solution)/shard_map/ppermute | solution.py:21
  126.0 4.8 %gather_fusion = f32[96,4,16,384]{3,2,1,0:T(8,128)} fusion(f32[24,4,16,384]{3,2,1,0:T(8,128)S(1)} %bitcast.62, s32[1024]{0:T(1024)S(1)} %pad_clamp_fusion.1), kind=kCustom, calls=%fused_computation | custom fusion | bytes 18874752 | tf_op jit(solution)/shard_map/gather | solution.py:118
  132.1 7.1 %all-to-all-start.2 = ((f32[8,12,4,16,384]{4,3,2,1,0:T(8,128)}), f32[8,12,4,16,384]{4,3,2,1,0:T(8,128)}, u32[]{:S(2)}, u32[]{:S(2)}) async-start(f32[8,12,4,16,384]{4,3,2,1,0:T(8,128)} %bitcast.63), calls=%async_computation.2 | async-start | bytes 18874368 | tf_op jit(solution)/shard_map/all_to_all | solution.py:119
  139.4 3.3 add.159
  142.7 201.9 %all-to-all-done.2 = f32[8,12,4,16,384]{4,3,2,1,0:T(8,128)} async-done(((f32[8,12,4,16,384]{4,3,2,1,0:T(8,128)}), f32[8,12,4,16,384]{4,3,2,1,0:T(8,128)}, u32[]{:S(2)}, u32[]{:S(2)}) %all-to-all-start.2) | async-done | bytes 9437216 | tf_op jit(solution)/shard_map/all_to_all | solution.py:119
  344.6 6.7 %gather_fusion.1 = f32[48,4,16,384]{3,2,1,0:T(8,128)} fusion(f32[96,4,16,384]{3,2,1,0:T(8,128)} %bitcast.18, s32[1024]{0:T(1024)S(1)} %pad_clamp_fusion), kind=kCustom, calls=%fused_computation.1 | custom fusion | bytes 9437376 | tf_op jit(solution)/shard_map/gather | solution.py:121
  351.4 2.9 fusion.2
  354.3 2.8 copy.77
  (95 shorter events, 29.4 us)
Async XLA Ops:
  0.6 10.0 %copy-start = (f32[4,16,24,384]{3,2,1,0:T(8,128)S(1)}, f32[4,16,24,384]{3,2,1,0:T(8,128)}, u32[]{:S(2)}) copy-start(f32[4,16,24,384]{3,2,1,0:T(8,128)} %param.8) | copy-start | bytes 7077892
  0.6 10.0 %copy-start.3 = (f32[16,24,384]{2,1,0:T(8,128)S(1)}, f32[16,24,384]{2,1,0:T(8,128)}, u32[]{:S(2)}) copy-start(f32[16,24,384]{2,1,0:T(8,128)} %param.10) | copy-start | bytes 1769476
  3.2 24.4 %collective-permute-start.2 = (f32[5,16,1,384]{3,1,2,0:T(8,128)}, f32[5,16,1,384]{3,1,2,0:T(8,128)}, u32[]{:S(2)}, u32[]{:S(2)}) collective-permute-start(f32[5,16,1,384]{3,1,2,0:T(8,128)} %copy.59), channel_id=1, source_target_pairs={{0,1},{1,2},{2,3},{3,4},{4,5},{5,6},{6,7},{8,9},{9,10},{10,11},{11... | collective-permute-start | bytes 368648 | tf_op jit(solution)/shard_map/ppermute | solution.py:33
  9.4 19.6 %collective-permute-start.3 = (f32[5,16,1,384]{3,1,2,0:T(8,128)}, f32[5,16,1,384]{3,1,2,0:T(8,128)}, u32[]{:S(2)}, u32[]{:S(2)}) collective-permute-start(f32[5,16,1,384]{3,1,2,0:T(8,128)} %copy.61), channel_id=1, source_target_pairs={{1,0},{2,1},{3,2},{4,3},{5,4},{6,5},{7,6},{9,8},{10,9},{11,10},{12... | collective-permute-start | bytes 368648 | tf_op jit(solution)/shard_map/ppermute | solution.py:34
  10.7 6.0 %copy-start.8 = (s32[24]{0:T(128)S(1)}, s32[24]{0:T(128)}, u32[]{:S(2)}) copy-start(s32[24]{0:T(128)} %param.12) | copy-start | bytes 292
  14.3 3.7 %collective-permute-start = (f32[5,16,24,1]{2,1,3,0:T(8,128)}, f32[5,16,24,1]{2,1,3,0:T(8,128)}, u32[]{:S(2)}, u32[]{:S(2)}) collective-permute-start(f32[5,16,24,1]{2,1,3,0:T(8,128)} %copy.55), channel_id=1, source_target_pairs={{0,8},{8,16},{16,24},{24,0},{1,9},{9,17},{17,25},{25,1},{2,10},{10... | collective-permute-start | bytes 23048 | tf_op jit(solution)/shard_map/ppermute | solution.py:33
  14.8 7.7 %collective-permute-start.1 = (f32[5,16,24,1]{2,1,3,0:T(8,128)S(1)}, f32[5,16,24,1]{2,1,3,0:T(8,128)}, u32[]{:S(2)}, u32[]{:S(2)}) collective-permute-start(f32[5,16,24,1]{2,1,3,0:T(8,128)S(1)} %copy.57), channel_id=1, source_target_pairs={{8,0},{16,8},{24,16},{0,24},{9,1},{17,9},{25,17},{1,25},{10,2},{18... | collective-permute-start | bytes 23048 | tf_op jit(solution)/shard_map/ppermute | solution.py:34
  24.8 3.8 %copy-start.4 = (f32[16,24,384]{2,1,0:T(8,128)S(1)}, f32[16,24,384]{2,1,0:T(8,128)}, u32[]{:S(2)}) copy-start(f32[16,24,384]{2,1,0:T(8,128)} %param.11) | copy-start | bytes 1769476
  33.4 32.1 %all-to-all-start = ((f32[4,384,384]{2,1,0:T(8,128)}), f32[4,384,384]{2,1,0:T(8,128)S(1)}, u32[]{:S(2)}, u32[]{:S(2)}) async-start(f32[4,384,384]{2,1,0:T(8,128)} %bitcast.64), calls=%async_computation | async-start | bytes 4718592 | tf_op jit(solution)/shard_map/all_to_all | solution.py:87
  71.2 14.8 %copy-start.1 = (f32[24,64,1536]{2,1,0:T(8,128)S(1)}, f32[24,64,1536]{2,1,0:T(8,128)}, u32[]{:S(2)}) copy-start(f32[24,64,1536]{2,1,0:T(8,128)} %add_select_fusion) | copy-start | bytes 28311556
  98.9 5.0 %copy-start.5 = (s32[24,2]{0,1:T(2,128)S(1)}, s32[24,2]{0,1:T(2,128)}, u32[]{:S(2)}) copy-start(s32[24,2]{0,1:T(2,128)} %param.13) | copy-start | bytes 580
  98.9 5.1 %copy-start.7 = (s32[24,2]{0,1:T(2,128)S(1)}, s32[24,2]{0,1:T(2,128)}, u32[]{:S(2)}) copy-start(s32[24,2]{0,1:T(2,128)} %param.14) | copy-start | bytes 580
  98.9 33.2 %all-to-all-start.1 = ((f32[384,4,384]{2,0,1:T(8,128)}), f32[384,4,384]{2,0,1:T(8,128)}, u32[]{:S(2)}, u32[]{:S(2)}) async-start(f32[384,4,384]{2,0,1:T(8,128)} %fusion.31), calls=%async_computation.1 | async-start | bytes 4718592 | tf_op jit(solution)/shard_map/all_to_all | solution.py:96
  104.9 10.8 %collective-permute-start.4 = (s32[1,12]{0,1:T(8,128)S(1)}, s32[1,12]{0,1:T(8,128)S(1)}, u32[]{:S(2)}, u32[]{:S(2)}) collective-permute-start(s32[1,12]{0,1:T(8,128)S(1)} %get-tuple-element.26), channel_id=1, source_target_pairs={{0,1},{1,0},{2,3},{3,2},{4,5},{5,4},{6,7},{7,6},{8,9},{9,8},{10,11... | collective-permute-start | bytes 152 | tf_op jit(solution)/shard_map/ppermute | solution.py:21
  107.5 11.9 %collective-permute-start.5 = (s32[1,12]{0,1:T(8,128)S(1)}, s32[1,12]{0,1:T(8,128)S(1)}, u32[]{:S(2)}, u32[]{:S(2)}) collective-permute-start(s32[1,12]{0,1:T(8,128)S(1)} %get-tuple-element.25), channel_id=1, source_target_pairs={{0,2},{1,3},{2,0},{3,1},{4,6},{5,7},{6,4},{7,5},{8,10},{9,11},{10,... | collective-permute-start | bytes 152 | tf_op jit(solution)/shard_map/ppermute | solution.py:21
  108.5 11.4 %collective-permute-start.6 = (s32[1,12]{0,1:T(8,128)S(1)}, s32[1,12]{0,1:T(8,128)S(1)}, u32[]{:S(2)}, u32[]{:S(2)}) collective-permute-start(s32[1,12]{0,1:T(8,128)S(1)} %get-tuple-element.24), channel_id=1, source_target_pairs={{0,3},{1,2},{2,1},{3,0},{4,7},{5,6},{6,5},{7,4},{8,11},{9,10},{10,... | collective-permute-start | bytes 152 | tf_op jit(solution)/shard_map/ppermute | solution.py:21
  109.3 10.6 %collective-permute-start.7 = (s32[1,12]{0,1:T(8,128)S(1)}, s32[1,12]{0,1:T(8,128)S(1)}, u32[]{:S(2)}, u32[]{:S(2)}) collective-permute-start(s32[1,12]{0,1:T(8,128)S(1)} %get-tuple-element.23), channel_id=1, source_target_pairs={{0,4},{1,5},{2,6},{3,7},{4,0},{5,1},{6,2},{7,3},{8,12},{9,13},{10,... | collective-permute-start | bytes 152 | tf_op jit(solution)/shard_map/ppermute | solution.py:21
  112.3 7.7 %collective-permute-start.8 = (s32[1,12]{0,1:T(8,128)S(1)}, s32[1,12]{0,1:T(8,128)S(1)}, u32[]{:S(2)}, u32[]{:S(2)}) collective-permute-start(s32[1,12]{0,1:T(8,128)S(1)} %get-tuple-element.22), channel_id=1, source_target_pairs={{0,5},{1,4},{2,7},{3,6},{4,1},{5,0},{6,3},{7,2},{8,13},{9,12},{10,... | collective-permute-start | bytes 152 | tf_op jit(solution)/shard_map/ppermute | solution.py:21
  115.7 5.5 %collective-permute-start.9 = (s32[1,12]{0,1:T(8,128)S(1)}, s32[1,12]{0,1:T(8,128)S(1)}, u32[]{:S(2)}, u32[]{:S(2)}) collective-permute-start(s32[1,12]{0,1:T(8,128)S(1)} %get-tuple-element.21), channel_id=1, source_target_pairs={{0,6},{1,7},{2,4},{3,5},{4,2},{5,3},{6,0},{7,1},{8,14},{9,15},{10,... | collective-permute-start | bytes 152 | tf_op jit(solution)/shard_map/ppermute | solution.py:21
  119.4 6.4 %collective-permute-start.10 = (s32[1,12]{0,1:T(8,128)S(1)}, s32[1,12]{0,1:T(8,128)S(1)}, u32[]{:S(2)}, u32[]{:S(2)}) collective-permute-start(s32[1,12]{0,1:T(8,128)S(1)} %get-tuple-element.20), channel_id=1, source_target_pairs={{0,7},{1,6},{2,5},{3,4},{4,3},{5,2},{6,1},{7,0},{8,15},{9,14},{10,... | collective-permute-start | bytes 152 | tf_op jit(solution)/shard_map/ppermute | solution.py:21
  132.1 7.3 %copy-start.6 = (f32[24,2]{0,1:T(2,128)S(1)}, f32[24,2]{0,1:T(2,128)}, u32[]{:S(2)}) copy-start(f32[24,2]{0,1:T(2,128)} %param.15) | copy-start | bytes 580
  132.1 7.3 %copy-start.2 = (f32[4,16,24,384]{3,2,1,0:T(8,128)S(1)}, f32[4,16,24,384]{3,2,1,0:T(8,128)}, u32[]{:S(2)}) copy-start(f32[4,16,24,384]{3,2,1,0:T(8,128)} %fusion.4) | copy-start | bytes 7077892
  132.1 212.5 %all-to-all-start.2 = ((f32[8,12,4,16,384]{4,3,2,1,0:T(8,128)}), f32[8,12,4,16,384]{4,3,2,1,0:T(8,128)}, u32[]{:S(2)}, u32[]{:S(2)}) async-start(f32[8,12,4,16,384]{4,3,2,1,0:T(8,128)} %bitcast.63), calls=%async_computation.2 | async-start | bytes 18874368 | tf_op jit(solution)/shard_map/all_to_all | solution.py:119
